TPU v7x, 32 devices: a whole 2x2x4 slice. The times are simulated.
32 devices in a mesh: batch: 8 (over z, y), width: 4 (over x, core).
Axes of the slice: x: 2, y: 2, z: 4, core: 2. Of those that a mesh axis runs over, the one named last changes fastest.
Arguments:
- teacher: bfloat16 [2048, 4096], P('batch', 'width'), may hold values from -48 to 48, as said below
- student: bfloat16 [2048, 1024], P('batch', 'width'), may hold values from -48 to 48, as said below
Outputs:
- grad: float32 [2048, 1024], P('batch', 'width')
Inputs may be any that keep to these rules, and one draw needn't show every extreme that they name: `teacher`: Real-valued embeddings. `student`: Real-valued embeddings.
All inputs are finite; a program needn't handle non-finite values.
Results may differ from a plain program's by a relative error of at most 0.00075.
Values may be sent and summed in bfloat16 or wider, within the bound.
No kernel may reach another device: no remote copies, remote signals or barrier semaphores. Data moves between devices by JAX's collectives and lax.ppermute only.
A program may use at most 64 MiB of HBM per device.

v0:
```python
import jax
import jax.numpy as jnp
from jax import lax
from jax.sharding import PartitionSpec as P


REACH = 4


def shifted(block, axis, distance):
    size = lax.axis_size(axis)
    route = [(i + distance, i) for i in range(size) if 0 <= i + distance < size]
    return lax.ppermute(block, axis, route)


def swapped(block, axis, mask):
    size = lax.axis_size(axis)
    return lax.ppermute(block, axis, [(i, i ^ mask) for i in range(size)])


def halves(x, axis, bit):
    half = x.shape[axis] // 2
    mine = (lax.axis_index("width") // bit) % 2
    keep = lax.dynamic_slice_in_dim(x, mine * half, half, axis)
    send = lax.dynamic_slice_in_dim(x, (1 - mine) * half, half, axis)
    return keep, send, mine


def joined(keep, got, axis, mine):
    first = jnp.where(mine == 0, keep, got)
    second = jnp.where(mine == 0, got, keep)
    return jnp.concatenate([first, second], axis=axis)


def width_sum(x):
    width = lax.axis_size("width")
    if width != 4:
        return lax.psum(x, "width")
    keep, send, core = halves(x, 2, 1)
    part = keep + swapped(send, "width", 1)
    keep, send, chip = halves(part, 1, 2)
    part = keep + swapped(send, "width", 2)
    part = joined(part, swapped(part, "width", 2), 1, chip)
    return joined(part, swapped(part, "width", 1), 2, core)


def layer(teacher, student):
    group = lax.axis_size("batch")
    owner = lax.axis_index("batch")
    width = lax.axis_size("width")
    rows_dev = teacher.shape[0]
    ft = teacher.shape[1]
    fs = student.shape[1]
    dt = ft * width
    ds = fs * width
    reach = min(REACH, group - 1)
    near_count = (2 * REACH + 1) * rows_dev

    def sq(x):
        xf = x.astype(jnp.float32)
        return jnp.sum(xf * xf, axis=1)

    offsets = [0] + [d if d % 2 else -d for d in range(1, reach + 1)]
    scaled = jnp.concatenate([teacher * jnp.bfloat16(-2.0 / dt), student * jnp.bfloat16(2.0 / ds)], axis=1)
    rhs_band = [scaled]
    for e in offsets[1:]:
        rhs_band.append(shifted(scaled, "batch", e))
    both = jnp.concatenate([teacher, student], axis=1)
    q_band = [sq(student) / ds - sq(teacher) / dt]
    q_band += [sq(b[:, ft:]) * (ds / 4.0) - sq(b[:, :ft]) * (dt / 4.0) for b in rhs_band[1:]]
    student_band = [student] + [b[:, ft:] for b in rhs_band[1:]]

    pad = (-(rows_dev + 1)) % 8

    def tile_part(d):
        g = lax.dot_general(both, rhs_band[d], (((1,), (1,)), ((), ())), preferred_element_type=jnp.float32)
        rows = jnp.zeros((pad + (8 if d == 0 else 0), rows_dev), jnp.float32)
        return jnp.concatenate([g, q_band[d][None, :], rows], axis=0)

    student_f = student.astype(jnp.float32)
    row_total = jnp.zeros((rows_dev,), jnp.float32)
    pulled = jnp.zeros(student.shape, jnp.float32)
    pulled_band = jnp.zeros(student.shape, jnp.float32)
    pulled_t = jnp.zeros((fs, rows_dev), jnp.float32)
    student_t = student.T
    own_q = None
    split = min(3, len(offsets))
    for group_idx in ([[0], list(range(1, split)), list(range(split, len(offsets)))]):
        if not group_idx:
            continue
        total = width_sum(jnp.stack([tile_part(d) for d in group_idx]))
        if own_q is None:
            own_q = total[0, rows_dev, :]
        for k, d in enumerate(group_idx):
            e = offsets[d]
            resid = own_q[:, None] + total[k, rows_dev, :][None, :] - total[k, :rows_dev, :]
            if d > 0:
                valid = jnp.logical_and(owner + e >= 0, owner + e < group)
                resid = jnp.where(valid, resid, jnp.zeros_like(resid))
            low = resid.astype(jnp.bfloat16)
            row_total = row_total + jnp.sum(resid, axis=1)
            if d == 0:
                pulled = pulled + jnp.dot(low, student_band[d], preferred_element_type=jnp.float32)
            else:
                pulled_band = pulled_band + jnp.dot(low, student_band[d], preferred_element_type=jnp.float32)
            if d > 0:
                col = jnp.sum(resid, axis=0)
                if fs == rows_dev:
                    back_t = jnp.dot(student_t, low, preferred_element_type=jnp.float32)
                    got = shifted(jnp.concatenate([back_t, col[None, :]], axis=0), "batch", -e)
                    pulled_t = pulled_t + got[:fs]
                    row_total = row_total + got[fs]
                else:
                    back = lax.dot_general(low, student, (((0,), (0,)), ((), ())), preferred_element_type=jnp.float32)
                    back_r, col_r = shifted((back, col), "batch", -e)
                    pulled = pulled + back_r
                    row_total = row_total + col_r
    pulled = pulled + pulled_band * (ds / 2.0)
    if fs == rows_dev:
        pulled = pulled + pulled_t.T
    grad = (student_f * row_total[:, None] - pulled) / near_count
    return grad


def solution(mesh):
    in_specs = (P("batch", "width"), P("batch", "width"))
    out_specs = P("batch", "width")
    return jax.shard_map(layer, mesh=mesh, in_specs=in_specs, out_specs=out_specs, check_vma=False)
```

profile of v0, /device:TPU:24, one launch (start us, length us, event | category | flops | bytes accessed | tf_op | source)
XLA Modules:
  0.0 102.1 jit_solution(3478319702324363170)
XLA Ops:
  0.0 1.3 %multiply_reduce_fusion.4 = f32[256]{0:T(256)S(1)} fusion(bf16[256,1024]{1,0:T(8,128)(2,1)} %param.2), kind=kLoop, calls=%fused_computation.14 | loop fusion | flops 786176 | bytes 525312 | tf_op jit(solution)/shard_map/reduce_sum | solution.py:61
  1.3 0.2 constant_dynamic-update-slice_fusion.1
  1.5 0.7 copy-done
  2.2 0.1 copy.3
  2.4 0.1 pad.38.clone
  2.5 0.4 fusion.55
  2.9 0.1 maximum_maximum_fusion
  3.1 1.3 %collective-permute-done = f32[1,272,128]{2,1,0:T(8,128)S(1)} collective-permute-done((f32[1,272,128]{2,1,0:T(8,128)S(1)}, f32[1,272,128]{2,1,0:T(8,128)S(1)}, u32[]{:S(2)}, u32[]{:S(2)}) %collective-permute-start) | collective-permute-done | bytes 139296 | tf_op jit(solution)/shard_map/ppermute | solution.py:18
  4.5 1.6 %collective-permute-start.1 = (f32[1,136,128]{2,1,0:T(8,128)S(1)}, f32[1,136,128]{2,1,0:T(8,128)S(1)}, u32[]{:S(2)}, u32[]{:S(2)}) collective-permute-start(f32[1,136,128]{2,1,0:T(8,128)S(1)} %constant_dynamic-slice_fusion.2), channel_id=1, source_target_pairs={{0,2},{1,3},{2,0},{3,1},{4,6},{5,7},{6,4},{7,5},{8,10},{9,11},{10,... | collective-permute-start | bytes 208904 | tf_op jit(solution)/shard_map/ppermute | solution.py:18
  6.0 2.8 %collective-permute-done.1 = f32[1,136,128]{2,1,0:T(8,128)S(1)} collective-permute-done((f32[1,136,128]{2,1,0:T(8,128)S(1)}, f32[1,136,128]{2,1,0:T(8,128)S(1)}, u32[]{:S(2)}, u32[]{:S(2)}) %collective-permute-start.1) | collective-permute-done | bytes 69664 | tf_op jit(solution)/shard_map/ppermute | solution.py:18
  8.9 1.6 %collective-permute-start.2 = (f32[1,136,128]{2,1,0:T(8,128)S(1)}, f32[1,136,128]{2,1,0:T(8,128)S(1)}, u32[]{:S(2)}, u32[]{:S(2)}) collective-permute-start(f32[1,136,128]{2,1,0:T(8,128)S(1)} %dynamic-slice_add_fusion.2), channel_id=1, source_target_pairs={{0,2},{1,3},{2,0},{3,1},{4,6},{5,7},{6,4},{7,5},{8,10},{9,11},{10,... | collective-permute-start | bytes 208904 | tf_op jit(solution)/shard_map/ppermute | solution.py:18
  10.4 0.9 pad_maximum_fusion
  11.3 3.2 %collective-permute-start.12 = (bf16[256,1280]{1,0:T(8,128)(2,1)}, bf16[256,1280]{1,0:T(8,128)(2,1)S(1)}, u32[]{:S(2)}, u32[]{:S(2)}) collective-permute-start(bf16[256,1280]{1,0:T(8,128)(2,1)} %pad_maximum_fusion), channel_id=1, source_target_pairs={{12,0},{16,4},{20,8},{24,12},{28,16},{13,1},{17,5},{21,9},{25,13},... | collective-permute-start | bytes 1966088 | tf_op jit(solution)/shard_map/ppermute | solution.py:13
  14.5 1.3 %collective-permute-start.5 = (bf16[256,1280]{1,0:T(8,128)(2,1)}, bf16[256,1280]{1,0:T(8,128)(2,1)S(1)}, u32[]{:S(2)}, u32[]{:S(2)}) collective-permute-start(bf16[256,1280]{1,0:T(8,128)(2,1)} %pad_maximum_fusion), channel_id=1, source_target_pairs={{0,8},{4,12},{8,16},{12,20},{16,24},{20,28},{1,9},{5,13},{9,17},{1... | collective-permute-start | bytes 1966088 | tf_op jit(solution)/shard_map/ppermute | solution.py:13
  15.9 0.7 pad_maximum_fusion.10
  16.6 4.6 %collective-permute-start.4 = (bf16[256,1280]{1,0:T(8,128)(2,1)}, bf16[256,1280]{1,0:T(8,128)(2,1)S(1)}, u32[]{:S(2)}, u32[]{:S(2)}) collective-permute-start(bf16[256,1280]{1,0:T(8,128)(2,1)} %pad_maximum_fusion), channel_id=1, source_target_pairs={{4,0},{8,4},{12,8},{16,12},{20,16},{24,20},{28,24},{5,1},{9,5},{13... | collective-permute-start | bytes 1966088 | tf_op jit(solution)/shard_map/ppermute | solution.py:13
  21.2 1.3 %collective-permute-start.13 = (bf16[256,1280]{1,0:T(8,128)(2,1)}, bf16[256,1280]{1,0:T(8,128)(2,1)S(1)}, u32[]{:S(2)}, u32[]{:S(2)}) collective-permute-start(bf16[256,1280]{1,0:T(8,128)(2,1)} %pad_maximum_fusion), channel_id=1, source_target_pairs={{0,16},{4,20},{8,24},{12,28},{1,17},{5,21},{9,25},{13,29},{2,18},{... | collective-permute-start | bytes 1966088 | tf_op jit(solution)/shard_map/ppermute | solution.py:13
  22.6 0.1 pad.31.clone
  22.6 1.0 broadcast_select_fusion.9
  23.7 6.3 %collective-permute-done.12 = bf16[256,1280]{1,0:T(8,128)(2,1)S(1)} collective-permute-done((bf16[256,1280]{1,0:T(8,128)(2,1)}, bf16[256,1280]{1,0:T(8,128)(2,1)S(1)}, u32[]{:S(2)}, u32[]{:S(2)}) %collective-permute-start.12) | collective-permute-done | bytes 655392 | tf_op jit(solution)/shard_map/ppermute | solution.py:13
  29.9 0.1 multiply_reduce_fusion.6
  30.0 2.1 %collective-permute-done.5 = bf16[256,1280]{1,0:T(8,128)(2,1)S(1)} collective-permute-done((bf16[256,1280]{1,0:T(8,128)(2,1)}, bf16[256,1280]{1,0:T(8,128)(2,1)S(1)}, u32[]{:S(2)}, u32[]{:S(2)}) %collective-permute-start.5) | collective-permute-done | bytes 655392 | tf_op jit(solution)/shard_map/ppermute | solution.py:13
  32.1 0.1 multiply_reduce_fusion.7
  32.3 0.2 multiply_reduce_fusion.1
  32.4 0.2 multiply_reduce_fusion.2
  32.6 9.1 %collective-permute-done.4 = bf16[256,1280]{1,0:T(8,128)(2,1)S(1)} collective-permute-done((bf16[256,1280]{1,0:T(8,128)(2,1)}, bf16[256,1280]{1,0:T(8,128)(2,1)S(1)}, u32[]{:S(2)}, u32[]{:S(2)}) %collective-permute-start.4) | collective-permute-done | bytes 655392 | tf_op jit(solution)/shard_map/ppermute | solution.py:13
  41.8 0.2 multiply_reduce_fusion.3
  41.9 0.1 multiply_reduce_fusion.8
  42.1 17.6 %collective-permute-done.13 = bf16[256,1280]{1,0:T(8,128)(2,1)S(1)} collective-permute-done((bf16[256,1280]{1,0:T(8,128)(2,1)}, bf16[256,1280]{1,0:T(8,128)(2,1)S(1)}, u32[]{:S(2)}, u32[]{:S(2)}) %collective-permute-start.13) | collective-permute-done | bytes 655392 | tf_op jit(solution)/shard_map/ppermute | solution.py:13
  59.7 0.2 multiply_reduce_fusion
  59.8 0.1 multiply_reduce_fusion.5
  60.0 0.4 fusion.66
  60.3 0.4 fusion.65
  60.7 0.4 fusion.64
  61.1 0.4 fusion.67
  61.4 0.1 maximum_bitcast_fusion.1
  61.7 0.3 fusion.33
  62.0 0.6 collective-permute-start.6
  62.6 0.6 collective-permute-done.14
  63.3 0.6 collective-permute-start.15
  64.0 1.6 %collective-permute-start.7 = (f32[2,132,128]{2,1,0:T(8,128)S(1)}, f32[2,132,128]{2,1,0:T(8,128)S(1)}, u32[]{:S(2)}, u32[]{:S(2)}) collective-permute-start(f32[2,132,128]{2,1,0:T(8,128)S(1)} %constant_dynamic-slice_fusion.1), channel_id=1, source_target_pairs={{0,2},{1,3},{2,0},{3,1},{4,6},{5,7},{6,4},{7,5},{8,10},{9,11},{10,... | collective-permute-start | bytes 405512 | tf_op jit(solution)/shard_map/ppermute | solution.py:18
  65.5 4.4 %collective-permute-done.15 = f32[2,132,128]{2,1,0:T(8,128)S(1)} collective-permute-done((f32[2,132,128]{2,1,0:T(8,128)S(1)}, f32[2,132,128]{2,1,0:T(8,128)S(1)}, u32[]{:S(2)}, u32[]{:S(2)}) %collective-permute-start.15) | collective-permute-done | bytes 135200 | tf_op jit(solution)/shard_map/ppermute | solution.py:18
  70.0 0.6 collective-permute-start.16
  70.6 2.4 %collective-permute-done.7 = f32[2,132,128]{2,1,0:T(8,128)S(1)} collective-permute-done((f32[2,132,128]{2,1,0:T(8,128)S(1)}, f32[2,132,128]{2,1,0:T(8,128)S(1)}, u32[]{:S(2)}, u32[]{:S(2)}) %collective-permute-start.7) | collective-permute-done | bytes 135200 | tf_op jit(solution)/shard_map/ppermute | solution.py:18
  72.9 0.6 collective-permute-start.8
  73.5 2.6 %collective-permute-done.16 = f32[2,132,128]{2,1,0:T(8,128)S(1)} collective-permute-done((f32[2,132,128]{2,1,0:T(8,128)S(1)}, f32[2,132,128]{2,1,0:T(8,128)S(1)}, u32[]{:S(2)}, u32[]{:S(2)}) %collective-permute-start.16) | collective-permute-done | bytes 135200 | tf_op jit(solution)/shard_map/ppermute | solution.py:18
  76.2 1.8 %collective-permute-done.8 = f32[2,132,128]{2,1,0:T(8,128)S(1)} collective-permute-done((f32[2,132,128]{2,1,0:T(8,128)S(1)}, f32[2,132,128]{2,1,0:T(8,128)S(1)}, u32[]{:S(2)}, u32[]{:S(2)}) %collective-permute-start.8) | collective-permute-done | bytes 135200 | tf_op jit(solution)/shard_map/ppermute | solution.py:18
  78.3 0.3 fusion.58
  78.6 0.2 convolution_bitcast_fusion
  78.8 1.6 %collective-permute-start.19 = (f32[257,256]{1,0:T(8,128)S(1)}, f32[257,256]{1,0:T(8,128)S(1)}, u32[]{:S(2)}, u32[]{:S(2)}) collective-permute-start(f32[257,256]{1,0:T(8,128)S(1)} %pad_maximum_fusion.6), channel_id=1, source_target_pairs={{16,0},{20,4},{24,8},{28,12},{17,1},{21,5},{25,9},{29,13},{18,2},{... | collective-permute-start | bytes 789512 | tf_op jit(solution)/shard_map/ppermute | solution.py:13
  80.4 0.2 convolution_bitcast_fusion.1
  80.7 1.3 %collective-permute-start.18 = (f32[257,256]{1,0:T(8,128)S(1)}, f32[257,256]{1,0:T(8,128)S(1)}, u32[]{:S(2)}, u32[]{:S(2)}) collective-permute-start(f32[257,256]{1,0:T(8,128)S(1)} %pad_maximum_fusion.5), channel_id=1, source_target_pairs={{0,12},{4,16},{8,20},{12,24},{16,28},{1,13},{5,17},{9,21},{13,25},... | collective-permute-start | bytes 789512 | tf_op jit(solution)/shard_map/ppermute | solution.py:13
  82.0 0.3 fusion.56
  82.3 0.2 convolution_bitcast_fusion.3
  82.5 0.2 convolution_bitcast_fusion.2
  82.8 4.7 %collective-permute-start.11 = (f32[257,256]{1,0:T(8,128)S(1)}, f32[257,256]{1,0:T(8,128)S(1)}, u32[]{:S(2)}, u32[]{:S(2)}) collective-permute-start(f32[257,256]{1,0:T(8,128)S(1)} %pad_maximum_fusion.3), channel_id=1, source_target_pairs={{8,0},{12,4},{16,8},{20,12},{24,16},{28,20},{9,1},{13,5},{17,9},{2... | collective-permute-start | bytes 789512 | tf_op jit(solution)/shard_map/ppermute | solution.py:13
  87.5 1.9 %collective-permute-start.10 = (f32[257,256]{1,0:T(8,128)S(1)}, f32[257,256]{1,0:T(8,128)S(1)}, u32[]{:S(2)}, u32[]{:S(2)}) collective-permute-start(f32[257,256]{1,0:T(8,128)S(1)} %pad_maximum_fusion.2), channel_id=1, source_target_pairs={{0,4},{4,8},{8,12},{12,16},{16,20},{20,24},{24,28},{1,5},{5,9},{9,... | collective-permute-start | bytes 789512 | tf_op jit(solution)/shard_map/ppermute | solution.py:13
  89.4 0.2 fusion.37
  89.7 0.2 fusion.39
  89.9 0.2 fusion.41
  90.1 5.1 %collective-permute-done.18 = f32[257,256]{1,0:T(8,128)S(1)} collective-permute-done((f32[257,256]{1,0:T(8,128)S(1)}, f32[257,256]{1,0:T(8,128)S(1)}, u32[]{:S(2)}, u32[]{:S(2)}) %collective-permute-start.18) | collective-permute-done | bytes 263200 | tf_op jit(solution)/shard_map/ppermute | solution.py:13
  95.3 5.7 %collective-permute-done.10 = f32[257,256]{1,0:T(8,128)S(1)} collective-permute-done((f32[257,256]{1,0:T(8,128)S(1)}, f32[257,256]{1,0:T(8,128)S(1)}, u32[]{:S(2)}, u32[]{:S(2)}) %collective-permute-start.10) | collective-permute-done | bytes 263200 | tf_op jit(solution)/shard_map/ppermute | solution.py:13
  101.0 0.3 fusion.13
  101.3 0.8 copy.9
  (59 shorter events, 1.0 us)
Async XLA Ops:
  0.0 1.3 %copy-start.1 = (bf16[256,1024]{1,0:T(8,128)(2,1)S(1)}, bf16[256,1024]{1,0:T(8,128)(2,1)}, u32[]{:S(2)}) copy-start(bf16[256,1024]{1,0:T(8,128)(2,1)} %param.2) | copy-start | bytes 1572868
  1.3 0.9 copy-start
  3.0 1.4 %collective-permute-start = (f32[1,272,128]{2,1,0:T(8,128)S(1)}, f32[1,272,128]{2,1,0:T(8,128)S(1)}, u32[]{:S(2)}, u32[]{:S(2)}) collective-permute-start(f32[1,272,128]{2,1,0:T(8,128)S(1)} %dynamic-slice_bitcast_fusion), channel_id=1, source_target_pairs={{0,1},{1,0},{2,3},{3,2},{4,5},{5,4},{6,7},{7,6},{8,9},{9,8},{10,11... | collective-permute-start | bytes 417800 | tf_op jit(solution)/shard_map/ppermute | solution.py:18
  4.5 4.4 %collective-permute-start.1 = (f32[1,136,128]{2,1,0:T(8,128)S(1)}, f32[1,136,128]{2,1,0:T(8,128)S(1)}, u32[]{:S(2)}, u32[]{:S(2)}) collective-permute-start(f32[1,136,128]{2,1,0:T(8,128)S(1)} %constant_dynamic-slice_fusion.2), channel_id=1, source_target_pairs={{0,2},{1,3},{2,0},{3,1},{4,6},{5,7},{6,4},{7,5},{8,10},{9,11},{10,... | collective-permute-start | bytes 208904 | tf_op jit(solution)/shard_map/ppermute | solution.py:18
  8.9 7.0 %collective-permute-start.2 = (f32[1,136,128]{2,1,0:T(8,128)S(1)}, f32[1,136,128]{2,1,0:T(8,128)S(1)}, u32[]{:S(2)}, u32[]{:S(2)}) collective-permute-start(f32[1,136,128]{2,1,0:T(8,128)S(1)} %dynamic-slice_add_fusion.2), channel_id=1, source_target_pairs={{0,2},{1,3},{2,0},{3,1},{4,6},{5,7},{6,4},{7,5},{8,10},{9,11},{10,... | collective-permute-start | bytes 208904 | tf_op jit(solution)/shard_map/ppermute | solution.py:18
  11.3 18.6 %collective-permute-start.12 = (bf16[256,1280]{1,0:T(8,128)(2,1)}, bf16[256,1280]{1,0:T(8,128)(2,1)S(1)}, u32[]{:S(2)}, u32[]{:S(2)}) collective-permute-start(bf16[256,1280]{1,0:T(8,128)(2,1)} %pad_maximum_fusion), channel_id=1, source_target_pairs={{12,0},{16,4},{20,8},{24,12},{28,16},{13,1},{17,5},{21,9},{25,13},... | collective-permute-start | bytes 1966088 | tf_op jit(solution)/shard_map/ppermute | solution.py:13
  14.5 17.6 %collective-permute-start.5 = (bf16[256,1280]{1,0:T(8,128)(2,1)}, bf16[256,1280]{1,0:T(8,128)(2,1)S(1)}, u32[]{:S(2)}, u32[]{:S(2)}) collective-permute-start(bf16[256,1280]{1,0:T(8,128)(2,1)} %pad_maximum_fusion), channel_id=1, source_target_pairs={{0,8},{4,12},{8,16},{12,20},{16,24},{20,28},{1,9},{5,13},{9,17},{1... | collective-permute-start | bytes 1966088 | tf_op jit(solution)/shard_map/ppermute | solution.py:13
  15.9 0.7 copy-start.2
  15.9 0.7 copy-start.3
  16.6 6.0 %collective-permute-start.3 = (f32[1,272,128]{2,1,0:T(8,128)}, f32[1,272,128]{2,1,0:T(8,128)}, u32[]{:S(2)}, u32[]{:S(2)}) collective-permute-start(f32[1,272,128]{2,1,0:T(8,128)} %pad_maximum_fusion.10), channel_id=1, source_target_pairs={{0,1},{1,0},{2,3},{3,2},{4,5},{5,4},{6,7},{7,6},{8,9},{9,8},{10,11... | collective-permute-start | bytes 417800 | tf_op jit(solution)/shard_map/ppermute | solution.py:18
  16.6 25.2 %collective-permute-start.4 = (bf16[256,1280]{1,0:T(8,128)(2,1)}, bf16[256,1280]{1,0:T(8,128)(2,1)S(1)}, u32[]{:S(2)}, u32[]{:S(2)}) collective-permute-start(bf16[256,1280]{1,0:T(8,128)(2,1)} %pad_maximum_fusion), channel_id=1, source_target_pairs={{4,0},{8,4},{12,8},{16,12},{20,16},{24,20},{28,24},{5,1},{9,5},{13... | collective-permute-start | bytes 1966088 | tf_op jit(solution)/shard_map/ppermute | solution.py:13
  21.2 38.4 %collective-permute-start.13 = (bf16[256,1280]{1,0:T(8,128)(2,1)}, bf16[256,1280]{1,0:T(8,128)(2,1)S(1)}, u32[]{:S(2)}, u32[]{:S(2)}) collective-permute-start(bf16[256,1280]{1,0:T(8,128)(2,1)} %pad_maximum_fusion), channel_id=1, source_target_pairs={{0,16},{4,20},{8,24},{12,28},{1,17},{5,21},{9,25},{13,29},{2,18},{... | collective-permute-start | bytes 1966088 | tf_op jit(solution)/shard_map/ppermute | solution.py:13
  61.6 1.6 %collective-permute-start.14 = (f32[2,264,128]{2,1,0:T(8,128)S(1)}, f32[2,264,128]{2,1,0:T(8,128)S(1)}, u32[]{:S(2)}, u32[]{:S(2)}) collective-permute-start(f32[2,264,128]{2,1,0:T(8,128)S(1)} %fusion.5), channel_id=1, source_target_pairs={{0,1},{1,0},{2,3},{3,2},{4,5},{5,4},{6,7},{7,6},{8,9},{9,8},{10,11... | collective-permute-start | bytes 811016 | tf_op jit(solution)/shard_map/ppermute | solution.py:18
  62.0 1.9 %collective-permute-start.6 = (f32[2,264,128]{2,1,0:T(8,128)S(1)}, f32[2,264,128]{2,1,0:T(8,128)S(1)}, u32[]{:S(2)}, u32[]{:S(2)}) collective-permute-start(f32[2,264,128]{2,1,0:T(8,128)S(1)} %fusion.8), channel_id=1, source_target_pairs={{0,1},{1,0},{2,3},{3,2},{4,5},{5,4},{6,7},{7,6},{8,9},{9,8},{10,11... | collective-permute-start | bytes 811016 | tf_op jit(solution)/shard_map/ppermute | solution.py:18
  63.3 6.6 %collective-permute-start.15 = (f32[2,132,128]{2,1,0:T(8,128)S(1)}, f32[2,132,128]{2,1,0:T(8,128)S(1)}, u32[]{:S(2)}, u32[]{:S(2)}) collective-permute-start(f32[2,132,128]{2,1,0:T(8,128)S(1)} %constant_dynamic-slice_fusion), channel_id=1, source_target_pairs={{0,2},{1,3},{2,0},{3,1},{4,6},{5,7},{6,4},{7,5},{8,10},{9,11},{10,... | collective-permute-start | bytes 405512 | tf_op jit(solution)/shard_map/ppermute | solution.py:18
  64.0 8.9 %collective-permute-start.7 = (f32[2,132,128]{2,1,0:T(8,128)S(1)}, f32[2,132,128]{2,1,0:T(8,128)S(1)}, u32[]{:S(2)}, u32[]{:S(2)}) collective-permute-start(f32[2,132,128]{2,1,0:T(8,128)S(1)} %constant_dynamic-slice_fusion.1), channel_id=1, source_target_pairs={{0,2},{1,3},{2,0},{3,1},{4,6},{5,7},{6,4},{7,5},{8,10},{9,11},{10,... | collective-permute-start | bytes 405512 | tf_op jit(solution)/shard_map/ppermute | solution.py:18
  70.0 6.2 %collective-permute-start.16 = (f32[2,132,128]{2,1,0:T(8,128)S(1)}, f32[2,132,128]{2,1,0:T(8,128)S(1)}, u32[]{:S(2)}, u32[]{:S(2)}) collective-permute-start(f32[2,132,128]{2,1,0:T(8,128)S(1)} %dynamic-slice_add_fusion), channel_id=1, source_target_pairs={{0,2},{1,3},{2,0},{3,1},{4,6},{5,7},{6,4},{7,5},{8,10},{9,11},{10,... | collective-permute-start | bytes 405512 | tf_op jit(solution)/shard_map/ppermute | solution.py:18
  72.9 5.1 %collective-permute-start.8 = (f32[2,132,128]{2,1,0:T(8,128)S(1)}, f32[2,132,128]{2,1,0:T(8,128)S(1)}, u32[]{:S(2)}, u32[]{:S(2)}) collective-permute-start(f32[2,132,128]{2,1,0:T(8,128)S(1)} %dynamic-slice_add_fusion.1), channel_id=1, source_target_pairs={{0,2},{1,3},{2,0},{3,1},{4,6},{5,7},{6,4},{7,5},{8,10},{9,11},{10,... | collective-permute-start | bytes 405512 | tf_op jit(solution)/shard_map/ppermute | solution.py:18
  76.2 2.0 %collective-permute-start.17 = (f32[2,264,128]{2,1,0:T(8,128)S(1)}, f32[2,264,128]{2,1,0:T(8,128)S(1)}, u32[]{:S(2)}, u32[]{:S(2)}) collective-permute-start(f32[2,264,128]{2,1,0:T(8,128)S(1)} %pad_maximum_fusion.4), channel_id=1, source_target_pairs={{0,1},{1,0},{2,3},{3,2},{4,5},{5,4},{6,7},{7,6},{8,9},{9,8},{10,11... | collective-permute-start | bytes 811016 | tf_op jit(solution)/shard_map/ppermute | solution.py:18
  78.1 3.9 %collective-permute-start.9 = (f32[2,264,128]{2,1,0:T(8,128)S(1)}, f32[2,264,128]{2,1,0:T(8,128)S(1)}, u32[]{:S(2)}, u32[]{:S(2)}) collective-permute-start(f32[2,264,128]{2,1,0:T(8,128)S(1)} %pad_maximum_fusion.1), channel_id=1, source_target_pairs={{0,1},{1,0},{2,3},{3,2},{4,5},{5,4},{6,7},{7,6},{8,9},{9,8},{10,11... | collective-permute-start | bytes 811016 | tf_op jit(solution)/shard_map/ppermute | solution.py:18
  78.8 11.3 %collective-permute-start.19 = (f32[257,256]{1,0:T(8,128)S(1)}, f32[257,256]{1,0:T(8,128)S(1)}, u32[]{:S(2)}, u32[]{:S(2)}) collective-permute-start(f32[257,256]{1,0:T(8,128)S(1)} %pad_maximum_fusion.6), channel_id=1, source_target_pairs={{16,0},{20,4},{24,8},{28,12},{17,1},{21,5},{25,9},{29,13},{18,2},{... | collective-permute-start | bytes 789512 | tf_op jit(solution)/shard_map/ppermute | solution.py:13
  80.7 14.6 %collective-permute-start.18 = (f32[257,256]{1,0:T(8,128)S(1)}, f32[257,256]{1,0:T(8,128)S(1)}, u32[]{:S(2)}, u32[]{:S(2)}) collective-permute-start(f32[257,256]{1,0:T(8,128)S(1)} %pad_maximum_fusion.5), channel_id=1, source_target_pairs={{0,12},{4,16},{8,20},{12,24},{16,28},{1,13},{5,17},{9,21},{13,25},... | collective-permute-start | bytes 789512 | tf_op jit(solution)/shard_map/ppermute | solution.py:13
  82.8 12.5 %collective-permute-start.11 = (f32[257,256]{1,0:T(8,128)S(1)}, f32[257,256]{1,0:T(8,128)S(1)}, u32[]{:S(2)}, u32[]{:S(2)}) collective-permute-start(f32[257,256]{1,0:T(8,128)S(1)} %pad_maximum_fusion.3), channel_id=1, source_target_pairs={{8,0},{12,4},{16,8},{20,12},{24,16},{28,20},{9,1},{13,5},{17,9},{2... | collective-permute-start | bytes 789512 | tf_op jit(solution)/shard_map/ppermute | solution.py:13
  87.5 13.4 %collective-permute-start.10 = (f32[257,256]{1,0:T(8,128)S(1)}, f32[257,256]{1,0:T(8,128)S(1)}, u32[]{:S(2)}, u32[]{:S(2)}) collective-permute-start(f32[257,256]{1,0:T(8,128)S(1)} %pad_maximum_fusion.2), channel_id=1, source_target_pairs={{0,4},{4,8},{8,12},{12,16},{16,20},{20,24},{24,28},{1,5},{5,9},{9,... | collective-permute-start | bytes 789512 | tf_op jit(solution)/shard_map/ppermute | solution.py:13
where the time goes:
time: 103 us; the launch traced here: 102 us
  waiting for transfers between devices  61.7 us (60%)
  starting transfers between devices  27.2 us (26%)
  other arithmetic  6.63 us (6%)
  matrix products  4 us (4%)
  local copies, waits for them, and re-layouts  1.91 us (2%)
    ppermute x8, waiting for transfers between devices, shifted(): return lax.ppermute(block, axis, route)  45.8 us
    ppermute x8, starting transfers between devices, shifted(): return lax.ppermute(block, axis, route)  19.9 us
    ppermute x12, waiting for transfers between devices, swapped(): return lax.ppermute(block, axis, [(i, i ^ mask) for i in range(size)])  15.9 us
    ppermute x12, starting transfers between devices, swapped(): return lax.ppermute(block, axis, [(i, i ^ mask) for i in range(size)])  7.33 us
    reduce_sum x10, other arithmetic, sq(): return jnp.sum(xf * xf, axis=1)  2.53 us
  transfers between devices with their start and end apart: 20, of which 13 were waited for; matrix products, arithmetic and copies ran while one was open for 6% of the time, Pallas kernels for 0%

commit v1 on v0

--- a/solution.py
+++ b/solution.py
@@ -81,11 +81,10 @@
     row_total = jnp.zeros((rows_dev,), jnp.float32)
     pulled = jnp.zeros(student.shape, jnp.float32)
     pulled_band = jnp.zeros(student.shape, jnp.float32)
-    pulled_t = jnp.zeros((fs, rows_dev), jnp.float32)
-    student_t = student.T
     own_q = None
-    split = min(3, len(offsets))
-    for group_idx in ([[0], list(range(1, split)), list(range(split, len(offsets)))]):
+    pulls = [d for d in range(1, len(offsets)) if offsets[d] > 0]
+    pushes = [d for d in range(1, len(offsets)) if offsets[d] < 0]
+    for group_idx in ([[0], pulls, pushes]):
         if not group_idx:
             continue
         total = width_sum(jnp.stack([tile_part(d) for d in group_idx]))
@@ -104,20 +103,17 @@
             else:
                 pulled_band = pulled_band + jnp.dot(low, student_band[d], preferred_element_type=jnp.float32)
             if d > 0:
+                back = lax.dot_general(low, student, (((0,), (0,)), ((), ())), preferred_element_type=jnp.float32)
                 col = jnp.sum(resid, axis=0)
                 if fs == rows_dev:
-                    back_t = jnp.dot(student_t, low, preferred_element_type=jnp.float32)
-                    got = shifted(jnp.concatenate([back_t, col[None, :]], axis=0), "batch", -e)
-                    pulled_t = pulled_t + got[:fs]
-                    row_total = row_total + got[fs]
+                    got = shifted(jnp.concatenate([back, col[None, :]], axis=0), "batch", -e)
+                    pulled = pulled + got[:rows_dev]
+                    row_total = row_total + got[rows_dev]
                 else:
-                    back = lax.dot_general(low, student, (((0,), (0,)), ((), ())), preferred_element_type=jnp.float32)
                     back_r, col_r = shifted((back, col), "batch", -e)
                     pulled = pulled + back_r
                     row_total = row_total + col_r
     pulled = pulled + pulled_band * (ds / 2.0)
-    if fs == rows_dev:
-        pulled = pulled + pulled_t.T
     grad = (student_f * row_total[:, None] - pulled) / near_count
     return grad
 

time: 103 us -> 109 us (1.058)
  the two profiles are of different devices: /device:TPU:24 before, /device:TPU:17 now
where the time goes in v1:
time: 109 us; the launch traced here: 108 us
  waiting for transfers between devices  60.6 us (56%)
  starting transfers between devices  35.1 us (32%)
  other arithmetic  6.58 us (6%)
  matrix products  4.5 us (4%)
    ppermute x8, waiting for transfers between devices, shifted(): return lax.ppermute(block, axis, route)  48.9 us
    ppermute x8, starting transfers between devices, shifted(): return lax.ppermute(block, axis, route)  20.8 us
    ppermute x12, starting transfers between devices, swapped(): return lax.ppermute(block, axis, [(i, i ^ mask) for i in range(size)])  14.3 us
    ppermute x12, waiting for transfers between devices, swapped(): return lax.ppermute(block, axis, [(i, i ^ mask) for i in range(size)])  11.7 us
    reduce_sum x10, other arithmetic, sq(): return jnp.sum(xf * xf, axis=1)  2.59 us
  transfers between devices with their start and end apart: 20, of which 12 were waited for; matrix products, arithmetic and copies ran while one was open for 6% of the time, Pallas kernels for 0%

profile of v1, /device:TPU:17, one launch (start us, length us, event | category | flops | bytes accessed | tf_op | source)
XLA Modules:
  0.0 108.3 jit_solution(10215274573221257163)
XLA Ops:
  0.0 1.3 %multiply_reduce_fusion.4 = f32[256]{0:T(256)S(1)} fusion(bf16[256,1024]{1,0:T(8,128)(2,1)} %param.2), kind=kLoop, calls=%fused_computation.8 | loop fusion | flops 786176 | bytes 525312 | tf_op jit(solution)/shard_map/reduce_sum | solution.py:61
  1.3 0.2 constant_dynamic-update-slice_fusion.1
  1.5 0.7 copy-done
  2.2 0.1 fusion.9
  2.5 0.4 fusion.59
  2.8 0.1 maximum_maximum_fusion
  3.0 0.7 collective-permute-start
  3.7 1.0 collective-permute-done
  4.8 1.3 %collective-permute-start.1 = (f32[1,136,128]{2,1,0:T(8,128)S(1)}, f32[1,136,128]{2,1,0:T(8,128)S(1)}, u32[]{:S(2)}, u32[]{:S(2)}) collective-permute-start(f32[1,136,128]{2,1,0:T(8,128)S(1)} %constant_dynamic-slice_fusion.2), channel_id=1, source_target_pairs={{0,2},{1,3},{2,0},{3,1},{4,6},{5,7},{6,4},{7,5},{8,10},{9,11},{10,... | collective-permute-start | bytes 208904 | tf_op jit(solution)/shard_map/ppermute | solution.py:18
  6.0 1.9 %collective-permute-done.1 = f32[1,136,128]{2,1,0:T(8,128)S(1)} collective-permute-done((f32[1,136,128]{2,1,0:T(8,128)S(1)}, f32[1,136,128]{2,1,0:T(8,128)S(1)}, u32[]{:S(2)}, u32[]{:S(2)}) %collective-permute-start.1) | collective-permute-done | bytes 69664 | tf_op jit(solution)/shard_map/ppermute | solution.py:18
  8.0 1.3 %collective-permute-start.2 = (f32[1,136,128]{2,1,0:T(8,128)S(1)}, f32[1,136,128]{2,1,0:T(8,128)S(1)}, u32[]{:S(2)}, u32[]{:S(2)}) collective-permute-start(f32[1,136,128]{2,1,0:T(8,128)S(1)} %dynamic-slice_add_fusion.2), channel_id=1, source_target_pairs={{0,2},{1,3},{2,0},{3,1},{4,6},{5,7},{6,4},{7,5},{8,10},{9,11},{10,... | collective-permute-start | bytes 208904 | tf_op jit(solution)/shard_map/ppermute | solution.py:18
  9.3 0.9 pad_maximum_fusion
  10.2 3.2 %collective-permute-start.12 = (bf16[256,1280]{1,0:T(8,128)(2,1)}, bf16[256,1280]{1,0:T(8,128)(2,1)S(1)}, u32[]{:S(2)}, u32[]{:S(2)}) collective-permute-start(bf16[256,1280]{1,0:T(8,128)(2,1)} %pad_maximum_fusion), channel_id=1, source_target_pairs={{0,8},{4,12},{8,16},{12,20},{16,24},{20,28},{1,9},{5,13},{9,17},{1... | collective-permute-start | bytes 1966088 | tf_op jit(solution)/shard_map/ppermute | solution.py:13
  13.4 3.0 %collective-permute-start.5 = (bf16[256,1280]{1,0:T(8,128)(2,1)}, bf16[256,1280]{1,0:T(8,128)(2,1)S(1)}, u32[]{:S(2)}, u32[]{:S(2)}) collective-permute-start(bf16[256,1280]{1,0:T(8,128)(2,1)} %pad_maximum_fusion), channel_id=1, source_target_pairs={{12,0},{16,4},{20,8},{24,12},{28,16},{13,1},{17,5},{21,9},{25,13},... | collective-permute-start | bytes 1966088 | tf_op jit(solution)/shard_map/ppermute | solution.py:13
  16.4 0.7 pad_maximum_fusion.10
  17.0 2.4 %collective-permute-start.3 = (f32[1,272,128]{2,1,0:T(8,128)}, f32[1,272,128]{2,1,0:T(8,128)}, u32[]{:S(2)}, u32[]{:S(2)}) collective-permute-start(f32[1,272,128]{2,1,0:T(8,128)} %pad_maximum_fusion.10), channel_id=1, source_target_pairs={{0,1},{1,0},{2,3},{3,2},{4,5},{5,4},{6,7},{7,6},{8,9},{9,8},{10,11... | collective-permute-start | bytes 417800 | tf_op jit(solution)/shard_map/ppermute | solution.py:18
  19.4 2.1 %collective-permute-start.4 = (bf16[256,1280]{1,0:T(8,128)(2,1)}, bf16[256,1280]{1,0:T(8,128)(2,1)S(1)}, u32[]{:S(2)}, u32[]{:S(2)}) collective-permute-start(bf16[256,1280]{1,0:T(8,128)(2,1)} %pad_maximum_fusion), channel_id=1, source_target_pairs={{4,0},{8,4},{12,8},{16,12},{20,16},{24,20},{28,24},{5,1},{9,5},{13... | collective-permute-start | bytes 1966088 | tf_op jit(solution)/shard_map/ppermute | solution.py:13
  21.5 1.3 %collective-permute-start.13 = (bf16[256,1280]{1,0:T(8,128)(2,1)}, bf16[256,1280]{1,0:T(8,128)(2,1)S(1)}, u32[]{:S(2)}, u32[]{:S(2)}) collective-permute-start(bf16[256,1280]{1,0:T(8,128)(2,1)} %pad_maximum_fusion), channel_id=1, source_target_pairs={{0,16},{4,20},{8,24},{12,28},{1,17},{5,21},{9,25},{13,29},{2,18},{... | collective-permute-start | bytes 1966088 | tf_op jit(solution)/shard_map/ppermute | solution.py:13
  22.9 0.9 broadcast_select_fusion.9
  23.9 2.9 %collective-permute-done.12 = bf16[256,1280]{1,0:T(8,128)(2,1)S(1)} collective-permute-done((bf16[256,1280]{1,0:T(8,128)(2,1)}, bf16[256,1280]{1,0:T(8,128)(2,1)S(1)}, u32[]{:S(2)}, u32[]{:S(2)}) %collective-permute-start.12) | collective-permute-done | bytes 655392 | tf_op jit(solution)/shard_map/ppermute | solution.py:13
  26.7 0.1 multiply_reduce_fusion.6
  26.9 17.3 %collective-permute-done.5 = bf16[256,1280]{1,0:T(8,128)(2,1)S(1)} collective-permute-done((bf16[256,1280]{1,0:T(8,128)(2,1)}, bf16[256,1280]{1,0:T(8,128)(2,1)S(1)}, u32[]{:S(2)}, u32[]{:S(2)}) %collective-permute-start.5) | collective-permute-done | bytes 655392 | tf_op jit(solution)/shard_map/ppermute | solution.py:13
  44.2 0.1 multiply_reduce_fusion.7
  44.3 0.2 multiply_reduce_fusion.1
  44.5 0.2 multiply_reduce_fusion.2
  44.7 13.6 %collective-permute-done.4 = bf16[256,1280]{1,0:T(8,128)(2,1)S(1)} collective-permute-done((bf16[256,1280]{1,0:T(8,128)(2,1)}, bf16[256,1280]{1,0:T(8,128)(2,1)S(1)}, u32[]{:S(2)}, u32[]{:S(2)}) %collective-permute-start.4) | collective-permute-done | bytes 655392 | tf_op jit(solution)/shard_map/ppermute | solution.py:13
  58.2 0.2 multiply_reduce_fusion.3
  58.4 0.1 multiply_reduce_fusion.8
  58.6 0.2 multiply_reduce_fusion
  58.8 0.1 multiply_reduce_fusion.5
  58.9 0.4 fusion.70
  59.3 0.4 fusion.69
  59.6 0.4 fusion.68
  60.0 0.4 fusion.71
  60.4 0.1 maximum_bitcast_fusion.1
  60.6 1.5 %collective-permute-start.14 = (f32[2,264,128]{2,1,0:T(8,128)S(1)}, f32[2,264,128]{2,1,0:T(8,128)S(1)}, u32[]{:S(2)}, u32[]{:S(2)}) collective-permute-start(f32[2,264,128]{2,1,0:T(8,128)S(1)} %fusion.3), channel_id=1, source_target_pairs={{0,1},{1,0},{2,3},{3,2},{4,5},{5,4},{6,7},{7,6},{8,9},{9,8},{10,11... | collective-permute-start | bytes 811016 | tf_op jit(solution)/shard_map/ppermute | solution.py:18
  62.1 0.2 fusion.31
  62.5 0.8 collective-permute-done.14
  63.3 0.3 collective-permute-start.15
  63.7 0.3 collective-permute-done.6
  64.1 1.0 collective-permute-start.7
  65.0 3.3 %collective-permute-done.15 = f32[2,132,128]{2,1,0:T(8,128)S(1)} collective-permute-done((f32[2,132,128]{2,1,0:T(8,128)S(1)}, f32[2,132,128]{2,1,0:T(8,128)S(1)}, u32[]{:S(2)}, u32[]{:S(2)}) %collective-permute-start.15) | collective-permute-done | bytes 135200 | tf_op jit(solution)/shard_map/ppermute | solution.py:18
  68.3 0.3 collective-permute-start.16
  68.6 2.6 %collective-permute-done.7 = f32[2,132,128]{2,1,0:T(8,128)S(1)} collective-permute-done((f32[2,132,128]{2,1,0:T(8,128)S(1)}, f32[2,132,128]{2,1,0:T(8,128)S(1)}, u32[]{:S(2)}, u32[]{:S(2)}) %collective-permute-start.7) | collective-permute-done | bytes 135200 | tf_op jit(solution)/shard_map/ppermute | solution.py:18
  71.3 0.3 collective-permute-start.8
  71.6 1.7 %collective-permute-done.16 = f32[2,132,128]{2,1,0:T(8,128)S(1)} collective-permute-done((f32[2,132,128]{2,1,0:T(8,128)S(1)}, f32[2,132,128]{2,1,0:T(8,128)S(1)}, u32[]{:S(2)}, u32[]{:S(2)}) %collective-permute-start.16) | collective-permute-done | bytes 135200 | tf_op jit(solution)/shard_map/ppermute | solution.py:18
  73.3 3.3 %collective-permute-start.17 = (f32[2,264,128]{2,1,0:T(8,128)S(1)}, f32[2,264,128]{2,1,0:T(8,128)S(1)}, u32[]{:S(2)}, u32[]{:S(2)}) collective-permute-start(f32[2,264,128]{2,1,0:T(8,128)S(1)} %pad_maximum_fusion.4), channel_id=1, source_target_pairs={{0,1},{1,0},{2,3},{3,2},{4,5},{5,4},{6,7},{7,6},{8,9},{9,8},{10,11... | collective-permute-start | bytes 811016 | tf_op jit(solution)/shard_map/ppermute | solution.py:18
  76.7 1.9 %collective-permute-start.9 = (f32[2,264,128]{2,1,0:T(8,128)S(1)}, f32[2,264,128]{2,1,0:T(8,128)S(1)}, u32[]{:S(2)}, u32[]{:S(2)}) collective-permute-start(f32[2,264,128]{2,1,0:T(8,128)S(1)} %pad_maximum_fusion.1), channel_id=1, source_target_pairs={{0,1},{1,0},{2,3},{3,2},{4,5},{5,4},{6,7},{7,6},{8,9},{9,8},{10,11... | collective-permute-start | bytes 811016 | tf_op jit(solution)/shard_map/ppermute | solution.py:18
  78.6 0.3 fusion.62
  78.9 0.2 fusion.45
  79.2 1.3 %collective-permute-start.19 = (f32[257,256]{1,0:T(8,128)S(1)}, f32[257,256]{1,0:T(8,128)S(1)}, u32[]{:S(2)}, u32[]{:S(2)}) collective-permute-start(f32[257,256]{1,0:T(8,128)S(1)} %pad_maximum_fusion.6), channel_id=1, source_target_pairs={{16,0},{20,4},{24,8},{28,12},{17,1},{21,5},{25,9},{29,13},{18,2},{... | collective-permute-start | bytes 789512 | tf_op jit(solution)/shard_map/ppermute | solution.py:13
  80.5 0.2 fusion.48
  80.8 1.9 %collective-permute-start.18 = (f32[257,256]{1,0:T(8,128)S(1)}, f32[257,256]{1,0:T(8,128)S(1)}, u32[]{:S(2)}, u32[]{:S(2)}) collective-permute-start(f32[257,256]{1,0:T(8,128)S(1)} %pad_maximum_fusion.5), channel_id=1, source_target_pairs={{8,0},{12,4},{16,8},{20,12},{24,16},{28,20},{9,1},{13,5},{17,9},{2... | collective-permute-start | bytes 789512 | tf_op jit(solution)/shard_map/ppermute | solution.py:13
  82.8 0.3 fusion.60
  83.0 0.2 fusion.54
  83.3 0.2 fusion.51
  83.5 6.1 %collective-permute-start.11 = (f32[257,256]{1,0:T(8,128)S(1)}, f32[257,256]{1,0:T(8,128)S(1)}, u32[]{:S(2)}, u32[]{:S(2)}) collective-permute-start(f32[257,256]{1,0:T(8,128)S(1)} %pad_maximum_fusion.3), channel_id=1, source_target_pairs={{0,12},{4,16},{8,20},{12,24},{16,28},{1,13},{5,17},{9,21},{13,25},... | collective-permute-start | bytes 789512 | tf_op jit(solution)/shard_map/ppermute | solution.py:13
  89.6 1.9 %collective-permute-start.10 = (f32[257,256]{1,0:T(8,128)S(1)}, f32[257,256]{1,0:T(8,128)S(1)}, u32[]{:S(2)}, u32[]{:S(2)}) collective-permute-start(f32[257,256]{1,0:T(8,128)S(1)} %pad_maximum_fusion.2), channel_id=1, source_target_pairs={{0,4},{4,8},{8,12},{12,16},{16,20},{20,24},{24,28},{1,5},{5,9},{9,... | collective-permute-start | bytes 789512 | tf_op jit(solution)/shard_map/ppermute | solution.py:13
  91.6 0.2 fusion.35
  91.8 0.2 fusion.37
  92.0 0.2 fusion.39
  92.2 4.5 %collective-permute-done.18 = f32[257,256]{1,0:T(8,128)S(1)} collective-permute-done((f32[257,256]{1,0:T(8,128)S(1)}, f32[257,256]{1,0:T(8,128)S(1)}, u32[]{:S(2)}, u32[]{:S(2)}) %collective-permute-start.18) | collective-permute-done | bytes 263200 | tf_op jit(solution)/shard_map/ppermute | solution.py:13
  96.7 10.6 %collective-permute-done.10 = f32[257,256]{1,0:T(8,128)S(1)} collective-permute-done((f32[257,256]{1,0:T(8,128)S(1)}, f32[257,256]{1,0:T(8,128)S(1)}, u32[]{:S(2)}, u32[]{:S(2)}) %collective-permute-start.10) | collective-permute-done | bytes 263200 | tf_op jit(solution)/shard_map/ppermute | solution.py:13
  107.3 1.0 fusion.11
  (53 shorter events, 0.9 us)
Async XLA Ops:
  0.0 1.3 %copy-start.1 = (bf16[256,1024]{1,0:T(8,128)(2,1)S(1)}, bf16[256,1024]{1,0:T(8,128)(2,1)}, u32[]{:S(2)}) copy-start(bf16[256,1024]{1,0:T(8,128)(2,1)} %param.2) | copy-start | bytes 1572868
  1.3 0.9 copy-start
  3.0 1.7 %collective-permute-start = (f32[1,272,128]{2,1,0:T(8,128)S(1)}, f32[1,272,128]{2,1,0:T(8,128)S(1)}, u32[]{:S(2)}, u32[]{:S(2)}) collective-permute-start(f32[1,272,128]{2,1,0:T(8,128)S(1)} %dynamic-slice_bitcast_fusion), channel_id=1, source_target_pairs={{0,1},{1,0},{2,3},{3,2},{4,5},{5,4},{6,7},{7,6},{8,9},{9,8},{10,11... | collective-permute-start | bytes 417800 | tf_op jit(solution)/shard_map/ppermute | solution.py:18
  4.8 3.2 %collective-permute-start.1 = (f32[1,136,128]{2,1,0:T(8,128)S(1)}, f32[1,136,128]{2,1,0:T(8,128)S(1)}, u32[]{:S(2)}, u32[]{:S(2)}) collective-permute-start(f32[1,136,128]{2,1,0:T(8,128)S(1)} %constant_dynamic-slice_fusion.2), channel_id=1, source_target_pairs={{0,2},{1,3},{2,0},{3,1},{4,6},{5,7},{6,4},{7,5},{8,10},{9,11},{10,... | collective-permute-start | bytes 208904 | tf_op jit(solution)/shard_map/ppermute | solution.py:18
  8.0 8.3 %collective-permute-start.2 = (f32[1,136,128]{2,1,0:T(8,128)S(1)}, f32[1,136,128]{2,1,0:T(8,128)S(1)}, u32[]{:S(2)}, u32[]{:S(2)}) collective-permute-start(f32[1,136,128]{2,1,0:T(8,128)S(1)} %dynamic-slice_add_fusion.2), channel_id=1, source_target_pairs={{0,2},{1,3},{2,0},{3,1},{4,6},{5,7},{6,4},{7,5},{8,10},{9,11},{10,... | collective-permute-start | bytes 208904 | tf_op jit(solution)/shard_map/ppermute | solution.py:18
  10.2 16.6 %collective-permute-start.12 = (bf16[256,1280]{1,0:T(8,128)(2,1)}, bf16[256,1280]{1,0:T(8,128)(2,1)S(1)}, u32[]{:S(2)}, u32[]{:S(2)}) collective-permute-start(bf16[256,1280]{1,0:T(8,128)(2,1)} %pad_maximum_fusion), channel_id=1, source_target_pairs={{0,8},{4,12},{8,16},{12,20},{16,24},{20,28},{1,9},{5,13},{9,17},{1... | collective-permute-start | bytes 1966088 | tf_op jit(solution)/shard_map/ppermute | solution.py:13
  13.4 30.8 %collective-permute-start.5 = (bf16[256,1280]{1,0:T(8,128)(2,1)}, bf16[256,1280]{1,0:T(8,128)(2,1)S(1)}, u32[]{:S(2)}, u32[]{:S(2)}) collective-permute-start(bf16[256,1280]{1,0:T(8,128)(2,1)} %pad_maximum_fusion), channel_id=1, source_target_pairs={{12,0},{16,4},{20,8},{24,12},{28,16},{13,1},{17,5},{21,9},{25,13},... | collective-permute-start | bytes 1966088 | tf_op jit(solution)/shard_map/ppermute | solution.py:13
  17.0 5.9 %collective-permute-start.3 = (f32[1,272,128]{2,1,0:T(8,128)}, f32[1,272,128]{2,1,0:T(8,128)}, u32[]{:S(2)}, u32[]{:S(2)}) collective-permute-start(f32[1,272,128]{2,1,0:T(8,128)} %pad_maximum_fusion.10), channel_id=1, source_target_pairs={{0,1},{1,0},{2,3},{3,2},{4,5},{5,4},{6,7},{7,6},{8,9},{9,8},{10,11... | collective-permute-start | bytes 417800 | tf_op jit(solution)/shard_map/ppermute | solution.py:18
  19.4 38.9 %collective-permute-start.4 = (bf16[256,1280]{1,0:T(8,128)(2,1)}, bf16[256,1280]{1,0:T(8,128)(2,1)S(1)}, u32[]{:S(2)}, u32[]{:S(2)}) collective-permute-start(bf16[256,1280]{1,0:T(8,128)(2,1)} %pad_maximum_fusion), channel_id=1, source_target_pairs={{4,0},{8,4},{12,8},{16,12},{20,16},{24,20},{28,24},{5,1},{9,5},{13... | collective-permute-start | bytes 1966088 | tf_op jit(solution)/shard_map/ppermute | solution.py:13
  21.5 37.1 %collective-permute-start.13 = (bf16[256,1280]{1,0:T(8,128)(2,1)}, bf16[256,1280]{1,0:T(8,128)(2,1)S(1)}, u32[]{:S(2)}, u32[]{:S(2)}) collective-permute-start(bf16[256,1280]{1,0:T(8,128)(2,1)} %pad_maximum_fusion), channel_id=1, source_target_pairs={{0,16},{4,20},{8,24},{12,28},{1,17},{5,21},{9,25},{13,29},{2,18},{... | collective-permute-start | bytes 1966088 | tf_op jit(solution)/shard_map/ppermute | solution.py:13
  60.6 2.7 %collective-permute-start.14 = (f32[2,264,128]{2,1,0:T(8,128)S(1)}, f32[2,264,128]{2,1,0:T(8,128)S(1)}, u32[]{:S(2)}, u32[]{:S(2)}) collective-permute-start(f32[2,264,128]{2,1,0:T(8,128)S(1)} %fusion.3), channel_id=1, source_target_pairs={{0,1},{1,0},{2,3},{3,2},{4,5},{5,4},{6,7},{7,6},{8,9},{9,8},{10,11... | collective-permute-start | bytes 811016 | tf_op jit(solution)/shard_map/ppermute | solution.py:18
  62.4 1.6 %collective-permute-start.6 = (f32[2,264,128]{2,1,0:T(8,128)S(1)}, f32[2,264,128]{2,1,0:T(8,128)S(1)}, u32[]{:S(2)}, u32[]{:S(2)}) collective-permute-start(f32[2,264,128]{2,1,0:T(8,128)S(1)} %fusion.6), channel_id=1, source_target_pairs={{0,1},{1,0},{2,3},{3,2},{4,5},{5,4},{6,7},{7,6},{8,9},{9,8},{10,11... | collective-permute-start | bytes 811016 | tf_op jit(solution)/shard_map/ppermute | solution.py:18
  63.3 4.9 %collective-permute-start.15 = (f32[2,132,128]{2,1,0:T(8,128)S(1)}, f32[2,132,128]{2,1,0:T(8,128)S(1)}, u32[]{:S(2)}, u32[]{:S(2)}) collective-permute-start(f32[2,132,128]{2,1,0:T(8,128)S(1)} %constant_dynamic-slice_fusion), channel_id=1, source_target_pairs={{0,2},{1,3},{2,0},{3,1},{4,6},{5,7},{6,4},{7,5},{8,10},{9,11},{10,... | collective-permute-start | bytes 405512 | tf_op jit(solution)/shard_map/ppermute | solution.py:18
  64.1 7.2 %collective-permute-start.7 = (f32[2,132,128]{2,1,0:T(8,128)S(1)}, f32[2,132,128]{2,1,0:T(8,128)S(1)}, u32[]{:S(2)}, u32[]{:S(2)}) collective-permute-start(f32[2,132,128]{2,1,0:T(8,128)S(1)} %constant_dynamic-slice_fusion.1), channel_id=1, source_target_pairs={{0,2},{1,3},{2,0},{3,1},{4,6},{5,7},{6,4},{7,5},{8,10},{9,11},{10,... | collective-permute-start | bytes 405512 | tf_op jit(solution)/shard_map/ppermute | solution.py:18
  68.3 5.0 %collective-permute-start.16 = (f32[2,132,128]{2,1,0:T(8,128)S(1)}, f32[2,132,128]{2,1,0:T(8,128)S(1)}, u32[]{:S(2)}, u32[]{:S(2)}) collective-permute-start(f32[2,132,128]{2,1,0:T(8,128)S(1)} %dynamic-slice_add_fusion), channel_id=1, source_target_pairs={{0,2},{1,3},{2,0},{3,1},{4,6},{5,7},{6,4},{7,5},{8,10},{9,11},{10,... | collective-permute-start | bytes 405512 | tf_op jit(solution)/shard_map/ppermute | solution.py:18
  71.3 5.4 %collective-permute-start.8 = (f32[2,132,128]{2,1,0:T(8,128)S(1)}, f32[2,132,128]{2,1,0:T(8,128)S(1)}, u32[]{:S(2)}, u32[]{:S(2)}) collective-permute-start(f32[2,132,128]{2,1,0:T(8,128)S(1)} %dynamic-slice_add_fusion.1), channel_id=1, source_target_pairs={{0,2},{1,3},{2,0},{3,1},{4,6},{5,7},{6,4},{7,5},{8,10},{9,11},{10,... | collective-permute-start | bytes 405512 | tf_op jit(solution)/shard_map/ppermute | solution.py:18
  73.3 5.3 %collective-permute-start.17 = (f32[2,264,128]{2,1,0:T(8,128)S(1)}, f32[2,264,128]{2,1,0:T(8,128)S(1)}, u32[]{:S(2)}, u32[]{:S(2)}) collective-permute-start(f32[2,264,128]{2,1,0:T(8,128)S(1)} %pad_maximum_fusion.4), channel_id=1, source_target_pairs={{0,1},{1,0},{2,3},{3,2},{4,5},{5,4},{6,7},{7,6},{8,9},{9,8},{10,11... | collective-permute-start | bytes 811016 | tf_op jit(solution)/shard_map/ppermute | solution.py:18
  76.7 6.0 %collective-permute-start.9 = (f32[2,264,128]{2,1,0:T(8,128)S(1)}, f32[2,264,128]{2,1,0:T(8,128)S(1)}, u32[]{:S(2)}, u32[]{:S(2)}) collective-permute-start(f32[2,264,128]{2,1,0:T(8,128)S(1)} %pad_maximum_fusion.1), channel_id=1, source_target_pairs={{0,1},{1,0},{2,3},{3,2},{4,5},{5,4},{6,7},{7,6},{8,9},{9,8},{10,11... | collective-permute-start | bytes 811016 | tf_op jit(solution)/shard_map/ppermute | solution.py:18
  79.2 12.9 %collective-permute-start.19 = (f32[257,256]{1,0:T(8,128)S(1)}, f32[257,256]{1,0:T(8,128)S(1)}, u32[]{:S(2)}, u32[]{:S(2)}) collective-permute-start(f32[257,256]{1,0:T(8,128)S(1)} %pad_maximum_fusion.6), channel_id=1, source_target_pairs={{16,0},{20,4},{24,8},{28,12},{17,1},{21,5},{25,9},{29,13},{18,2},{... | collective-permute-start | bytes 789512 | tf_op jit(solution)/shard_map/ppermute | solution.py:13
  80.8 15.9 %collective-permute-start.18 = (f32[257,256]{1,0:T(8,128)S(1)}, f32[257,256]{1,0:T(8,128)S(1)}, u32[]{:S(2)}, u32[]{:S(2)}) collective-permute-start(f32[257,256]{1,0:T(8,128)S(1)} %pad_maximum_fusion.5), channel_id=1, source_target_pairs={{8,0},{12,4},{16,8},{20,12},{24,16},{28,20},{9,1},{13,5},{17,9},{2... | collective-permute-start | bytes 789512 | tf_op jit(solution)/shard_map/ppermute | solution.py:13
  83.5 13.1 %collective-permute-start.11 = (f32[257,256]{1,0:T(8,128)S(1)}, f32[257,256]{1,0:T(8,128)S(1)}, u32[]{:S(2)}, u32[]{:S(2)}) collective-permute-start(f32[257,256]{1,0:T(8,128)S(1)} %pad_maximum_fusion.3), channel_id=1, source_target_pairs={{0,12},{4,16},{8,20},{12,24},{16,28},{1,13},{5,17},{9,21},{13,25},... | collective-permute-start | bytes 789512 | tf_op jit(solution)/shard_map/ppermute | solution.py:13
  89.6 17.6 %collective-permute-start.10 = (f32[257,256]{1,0:T(8,128)S(1)}, f32[257,256]{1,0:T(8,128)S(1)}, u32[]{:S(2)}, u32[]{:S(2)}) collective-permute-start(f32[257,256]{1,0:T(8,128)S(1)} %pad_maximum_fusion.2), channel_id=1, source_target_pairs={{0,4},{4,8},{8,12},{12,16},{16,20},{20,24},{24,28},{1,5},{5,9},{9,... | collective-permute-start | bytes 789512 | tf_op jit(solution)/shard_map/ppermute | solution.py:13

commit v2 on v1

--- a/solution.py
+++ b/solution.py
@@ -82,9 +82,8 @@
     pulled = jnp.zeros(student.shape, jnp.float32)
     pulled_band = jnp.zeros(student.shape, jnp.float32)
     own_q = None
-    pulls = [d for d in range(1, len(offsets)) if offsets[d] > 0]
-    pushes = [d for d in range(1, len(offsets)) if offsets[d] < 0]
-    for group_idx in ([[0], pulls, pushes]):
+    split = min(3, len(offsets))
+    for group_idx in ([[0], list(range(split, len(offsets))), list(range(1, split))]):
         if not group_idx:
             continue
         total = width_sum(jnp.stack([tile_part(d) for d in group_idx]))

time: 109 us -> 107 us (0.982)
  the two profiles are of different devices: /device:TPU:17 before, /device:TPU:24 now
where the time goes in v2:
time: 107 us; the launch traced here: 106 us
  waiting for transfers between devices  61.5 us (57%)
  starting transfers between devices  32.1 us (30%)
  other arithmetic  6.58 us (6%)
  matrix products  4.5 us (4%)
    ppermute x8, waiting for transfers between devices, shifted(): return lax.ppermute(block, axis, route)  45.6 us
    ppermute x8, starting transfers between devices, shifted(): return lax.ppermute(block, axis, route)  24.8 us
    ppermute x12, waiting for transfers between devices, swapped(): return lax.ppermute(block, axis, [(i, i ^ mask) for i in range(size)])  16 us
    ppermute x12, starting transfers between devices, swapped(): return lax.ppermute(block, axis, [(i, i ^ mask) for i in range(size)])  7.31 us
    reduce_sum x10, other arithmetic, sq(): return jnp.sum(xf * xf, axis=1)  2.59 us
  transfers between devices with their start and end apart: 20, of which 13 were waited for; matrix products, arithmetic and copies ran while one was open for 6% of the time, Pallas kernels for 0%

profile of v2, /device:TPU:24, one launch (start us, length us, event | category | flops | bytes accessed | tf_op | source)
XLA Modules:
  0.0 106.3 jit_solution(1971669058070555544)
XLA Ops:
  0.0 1.3 %multiply_reduce_fusion.4 = f32[256]{0:T(256)S(1)} fusion(bf16[256,1024]{1,0:T(8,128)(2,1)} %param.2), kind=kLoop, calls=%fused_computation.8 | loop fusion | flops 786176 | bytes 525312 | tf_op jit(solution)/shard_map/reduce_sum | solution.py:61
  1.3 0.2 constant_dynamic-update-slice_fusion.1
  1.5 0.7 copy-done
  2.2 0.1 fusion.9
  2.4 0.1 pad.38.clone
  2.5 0.4 fusion.59
  2.8 0.1 maximum_maximum_fusion
  3.1 1.3 %collective-permute-done = f32[1,272,128]{2,1,0:T(8,128)S(1)} collective-permute-done((f32[1,272,128]{2,1,0:T(8,128)S(1)}, f32[1,272,128]{2,1,0:T(8,128)S(1)}, u32[]{:S(2)}, u32[]{:S(2)}) %collective-permute-start) | collective-permute-done | bytes 139296 | tf_op jit(solution)/shard_map/ppermute | solution.py:18
  4.5 1.6 %collective-permute-start.1 = (f32[1,136,128]{2,1,0:T(8,128)S(1)}, f32[1,136,128]{2,1,0:T(8,128)S(1)}, u32[]{:S(2)}, u32[]{:S(2)}) collective-permute-start(f32[1,136,128]{2,1,0:T(8,128)S(1)} %constant_dynamic-slice_fusion.2), channel_id=1, source_target_pairs={{0,2},{1,3},{2,0},{3,1},{4,6},{5,7},{6,4},{7,5},{8,10},{9,11},{10,... | collective-permute-start | bytes 208904 | tf_op jit(solution)/shard_map/ppermute | solution.py:18
  6.0 2.8 %collective-permute-done.1 = f32[1,136,128]{2,1,0:T(8,128)S(1)} collective-permute-done((f32[1,136,128]{2,1,0:T(8,128)S(1)}, f32[1,136,128]{2,1,0:T(8,128)S(1)}, u32[]{:S(2)}, u32[]{:S(2)}) %collective-permute-start.1) | collective-permute-done | bytes 69664 | tf_op jit(solution)/shard_map/ppermute | solution.py:18
  8.8 1.6 %collective-permute-start.2 = (f32[1,136,128]{2,1,0:T(8,128)S(1)}, f32[1,136,128]{2,1,0:T(8,128)S(1)}, u32[]{:S(2)}, u32[]{:S(2)}) collective-permute-start(f32[1,136,128]{2,1,0:T(8,128)S(1)} %dynamic-slice_add_fusion.2), channel_id=1, source_target_pairs={{0,2},{1,3},{2,0},{3,1},{4,6},{5,7},{6,4},{7,5},{8,10},{9,11},{10,... | collective-permute-start | bytes 208904 | tf_op jit(solution)/shard_map/ppermute | solution.py:18
  10.4 0.9 pad_maximum_fusion
  11.3 3.3 %collective-permute-start.12 = (bf16[256,1280]{1,0:T(8,128)(2,1)}, bf16[256,1280]{1,0:T(8,128)(2,1)S(1)}, u32[]{:S(2)}, u32[]{:S(2)}) collective-permute-start(bf16[256,1280]{1,0:T(8,128)(2,1)} %pad_maximum_fusion), channel_id=1, source_target_pairs={{4,0},{8,4},{12,8},{16,12},{20,16},{24,20},{28,24},{5,1},{9,5},{13... | collective-permute-start | bytes 1966088 | tf_op jit(solution)/shard_map/ppermute | solution.py:13
  14.6 1.3 %collective-permute-start.5 = (bf16[256,1280]{1,0:T(8,128)(2,1)}, bf16[256,1280]{1,0:T(8,128)(2,1)S(1)}, u32[]{:S(2)}, u32[]{:S(2)}) collective-permute-start(bf16[256,1280]{1,0:T(8,128)(2,1)} %pad_maximum_fusion), channel_id=1, source_target_pairs={{0,16},{4,20},{8,24},{12,28},{1,17},{5,21},{9,25},{13,29},{2,18},{... | collective-permute-start | bytes 1966088 | tf_op jit(solution)/shard_map/ppermute | solution.py:13
  15.9 0.7 pad_maximum_fusion.10
  16.6 5.6 %collective-permute-start.4 = (bf16[256,1280]{1,0:T(8,128)(2,1)}, bf16[256,1280]{1,0:T(8,128)(2,1)S(1)}, u32[]{:S(2)}, u32[]{:S(2)}) collective-permute-start(bf16[256,1280]{1,0:T(8,128)(2,1)} %pad_maximum_fusion), channel_id=1, source_target_pairs={{12,0},{16,4},{20,8},{24,12},{28,16},{13,1},{17,5},{21,9},{25,13},... | collective-permute-start | bytes 1966088 | tf_op jit(solution)/shard_map/ppermute | solution.py:13
  22.2 1.3 %collective-permute-start.13 = (bf16[256,1280]{1,0:T(8,128)(2,1)}, bf16[256,1280]{1,0:T(8,128)(2,1)S(1)}, u32[]{:S(2)}, u32[]{:S(2)}) collective-permute-start(bf16[256,1280]{1,0:T(8,128)(2,1)} %pad_maximum_fusion), channel_id=1, source_target_pairs={{0,8},{4,12},{8,16},{12,20},{16,24},{20,28},{1,9},{5,13},{9,17},{1... | collective-permute-start | bytes 1966088 | tf_op jit(solution)/shard_map/ppermute | solution.py:13
  23.5 0.1 pad.31.clone
  23.6 0.9 broadcast_select_fusion.9
  24.6 5.4 %collective-permute-done.12 = bf16[256,1280]{1,0:T(8,128)(2,1)S(1)} collective-permute-done((bf16[256,1280]{1,0:T(8,128)(2,1)}, bf16[256,1280]{1,0:T(8,128)(2,1)S(1)}, u32[]{:S(2)}, u32[]{:S(2)}) %collective-permute-start.12) | collective-permute-done | bytes 655392 | tf_op jit(solution)/shard_map/ppermute | solution.py:13
  30.0 0.1 multiply_reduce_fusion.6
  30.1 16.6 %collective-permute-done.5 = bf16[256,1280]{1,0:T(8,128)(2,1)S(1)} collective-permute-done((bf16[256,1280]{1,0:T(8,128)(2,1)}, bf16[256,1280]{1,0:T(8,128)(2,1)S(1)}, u32[]{:S(2)}, u32[]{:S(2)}) %collective-permute-start.5) | collective-permute-done | bytes 655392 | tf_op jit(solution)/shard_map/ppermute | solution.py:13
  46.7 0.1 multiply_reduce_fusion.7
  46.9 0.2 multiply_reduce_fusion.1
  47.0 0.2 multiply_reduce_fusion.2
  47.2 0.2 multiply_reduce_fusion.3
  47.4 0.1 multiply_reduce_fusion.8
  47.6 7.5 %collective-permute-done.13 = bf16[256,1280]{1,0:T(8,128)(2,1)S(1)} collective-permute-done((bf16[256,1280]{1,0:T(8,128)(2,1)}, bf16[256,1280]{1,0:T(8,128)(2,1)S(1)}, u32[]{:S(2)}, u32[]{:S(2)}) %collective-permute-start.13) | collective-permute-done | bytes 655392 | tf_op jit(solution)/shard_map/ppermute | solution.py:13
  55.1 0.2 multiply_reduce_fusion
  55.3 0.1 multiply_reduce_fusion.5
  55.4 0.4 fusion.70
  55.8 0.4 fusion.69
  56.2 0.4 fusion.68
  56.5 0.4 fusion.71
  56.9 0.1 maximum_bitcast_fusion.1
  57.1 0.1 collective-permute-start.14
  57.2 0.2 fusion.31
  57.4 0.6 collective-permute-start.6
  58.0 0.7 collective-permute-done.14
  58.8 0.6 collective-permute-start.15
  59.5 1.6 %collective-permute-start.7 = (f32[2,132,128]{2,1,0:T(8,128)S(1)}, f32[2,132,128]{2,1,0:T(8,128)S(1)}, u32[]{:S(2)}, u32[]{:S(2)}) collective-permute-start(f32[2,132,128]{2,1,0:T(8,128)S(1)} %constant_dynamic-slice_fusion.1), channel_id=1, source_target_pairs={{0,2},{1,3},{2,0},{3,1},{4,6},{5,7},{6,4},{7,5},{8,10},{9,11},{10,... | collective-permute-start | bytes 405512 | tf_op jit(solution)/shard_map/ppermute | solution.py:18
  61.0 4.4 %collective-permute-done.15 = f32[2,132,128]{2,1,0:T(8,128)S(1)} collective-permute-done((f32[2,132,128]{2,1,0:T(8,128)S(1)}, f32[2,132,128]{2,1,0:T(8,128)S(1)}, u32[]{:S(2)}, u32[]{:S(2)}) %collective-permute-start.15) | collective-permute-done | bytes 135200 | tf_op jit(solution)/shard_map/ppermute | solution.py:18
  65.4 0.6 collective-permute-start.16
  66.0 2.4 %collective-permute-done.7 = f32[2,132,128]{2,1,0:T(8,128)S(1)} collective-permute-done((f32[2,132,128]{2,1,0:T(8,128)S(1)}, f32[2,132,128]{2,1,0:T(8,128)S(1)}, u32[]{:S(2)}, u32[]{:S(2)}) %collective-permute-start.7) | collective-permute-done | bytes 135200 | tf_op jit(solution)/shard_map/ppermute | solution.py:18
  68.4 0.6 collective-permute-start.8
  69.0 2.6 %collective-permute-done.16 = f32[2,132,128]{2,1,0:T(8,128)S(1)} collective-permute-done((f32[2,132,128]{2,1,0:T(8,128)S(1)}, f32[2,132,128]{2,1,0:T(8,128)S(1)}, u32[]{:S(2)}, u32[]{:S(2)}) %collective-permute-start.16) | collective-permute-done | bytes 135200 | tf_op jit(solution)/shard_map/ppermute | solution.py:18
  71.7 1.8 %collective-permute-done.8 = f32[2,132,128]{2,1,0:T(8,128)S(1)} collective-permute-done((f32[2,132,128]{2,1,0:T(8,128)S(1)}, f32[2,132,128]{2,1,0:T(8,128)S(1)}, u32[]{:S(2)}, u32[]{:S(2)}) %collective-permute-start.8) | collective-permute-done | bytes 135200 | tf_op jit(solution)/shard_map/ppermute | solution.py:18
  73.7 0.3 fusion.62
  74.0 0.2 fusion.45
  74.3 8.1 %collective-permute-start.19 = (f32[257,256]{1,0:T(8,128)S(1)}, f32[257,256]{1,0:T(8,128)S(1)}, u32[]{:S(2)}, u32[]{:S(2)}) collective-permute-start(f32[257,256]{1,0:T(8,128)S(1)} %pad_maximum_fusion.6), channel_id=1, source_target_pairs={{8,0},{12,4},{16,8},{20,12},{24,16},{28,20},{9,1},{13,5},{17,9},{2... | collective-permute-start | bytes 789512 | tf_op jit(solution)/shard_map/ppermute | solution.py:13
  82.3 0.2 fusion.48
  82.6 2.5 %collective-permute-start.18 = (f32[257,256]{1,0:T(8,128)S(1)}, f32[257,256]{1,0:T(8,128)S(1)}, u32[]{:S(2)}, u32[]{:S(2)}) collective-permute-start(f32[257,256]{1,0:T(8,128)S(1)} %pad_maximum_fusion.5), channel_id=1, source_target_pairs={{0,4},{4,8},{8,12},{12,16},{16,20},{20,24},{24,28},{1,5},{5,9},{9,... | collective-permute-start | bytes 789512 | tf_op jit(solution)/shard_map/ppermute | solution.py:13
  85.2 0.3 fusion.60
  85.5 0.2 fusion.54
  85.7 0.2 fusion.51
  86.0 1.4 %collective-permute-start.11 = (f32[257,256]{1,0:T(8,128)S(1)}, f32[257,256]{1,0:T(8,128)S(1)}, u32[]{:S(2)}, u32[]{:S(2)}) collective-permute-start(f32[257,256]{1,0:T(8,128)S(1)} %pad_maximum_fusion.3), channel_id=1, source_target_pairs={{16,0},{20,4},{24,8},{28,12},{17,1},{21,5},{25,9},{29,13},{18,2},{... | collective-permute-start | bytes 789512 | tf_op jit(solution)/shard_map/ppermute | solution.py:13
  87.4 1.3 %collective-permute-start.10 = (f32[257,256]{1,0:T(8,128)S(1)}, f32[257,256]{1,0:T(8,128)S(1)}, u32[]{:S(2)}, u32[]{:S(2)}) collective-permute-start(f32[257,256]{1,0:T(8,128)S(1)} %pad_maximum_fusion.2), channel_id=1, source_target_pairs={{0,12},{4,16},{8,20},{12,24},{16,28},{1,13},{5,17},{9,21},{13,25},... | collective-permute-start | bytes 789512 | tf_op jit(solution)/shard_map/ppermute | solution.py:13
  88.7 0.2 fusion.35
  88.9 0.2 fusion.37
  89.1 0.2 fusion.39
  89.3 4.7 %collective-permute-done.18 = f32[257,256]{1,0:T(8,128)S(1)} collective-permute-done((f32[257,256]{1,0:T(8,128)S(1)}, f32[257,256]{1,0:T(8,128)S(1)}, u32[]{:S(2)}, u32[]{:S(2)}) %collective-permute-start.18) | collective-permute-done | bytes 263200 | tf_op jit(solution)/shard_map/ppermute | solution.py:13
  94.0 0.5 collective-permute-done.11
  94.5 10.7 %collective-permute-done.10 = f32[257,256]{1,0:T(8,128)S(1)} collective-permute-done((f32[257,256]{1,0:T(8,128)S(1)}, f32[257,256]{1,0:T(8,128)S(1)}, u32[]{:S(2)}, u32[]{:S(2)}) %collective-permute-start.10) | collective-permute-done | bytes 263200 | tf_op jit(solution)/shard_map/ppermute | solution.py:13
  105.3 1.0 fusion.11
  (53 shorter events, 0.9 us)
Async XLA Ops:
  0.0 1.3 %copy-start.1 = (bf16[256,1024]{1,0:T(8,128)(2,1)S(1)}, bf16[256,1024]{1,0:T(8,128)(2,1)}, u32[]{:S(2)}) copy-start(bf16[256,1024]{1,0:T(8,128)(2,1)} %param.2) | copy-start | bytes 1572868
  1.3 0.9 copy-start
  3.0 1.4 %collective-permute-start = (f32[1,272,128]{2,1,0:T(8,128)S(1)}, f32[1,272,128]{2,1,0:T(8,128)S(1)}, u32[]{:S(2)}, u32[]{:S(2)}) collective-permute-start(f32[1,272,128]{2,1,0:T(8,128)S(1)} %dynamic-slice_bitcast_fusion), channel_id=1, source_target_pairs={{0,1},{1,0},{2,3},{3,2},{4,5},{5,4},{6,7},{7,6},{8,9},{9,8},{10,11... | collective-permute-start | bytes 417800 | tf_op jit(solution)/shard_map/ppermute | solution.py:18
  4.5 4.4 %collective-permute-start.1 = (f32[1,136,128]{2,1,0:T(8,128)S(1)}, f32[1,136,128]{2,1,0:T(8,128)S(1)}, u32[]{:S(2)}, u32[]{:S(2)}) collective-permute-start(f32[1,136,128]{2,1,0:T(8,128)S(1)} %constant_dynamic-slice_fusion.2), channel_id=1, source_target_pairs={{0,2},{1,3},{2,0},{3,1},{4,6},{5,7},{6,4},{7,5},{8,10},{9,11},{10,... | collective-permute-start | bytes 208904 | tf_op jit(solution)/shard_map/ppermute | solution.py:18
  8.8 7.0 %collective-permute-start.2 = (f32[1,136,128]{2,1,0:T(8,128)S(1)}, f32[1,136,128]{2,1,0:T(8,128)S(1)}, u32[]{:S(2)}, u32[]{:S(2)}) collective-permute-start(f32[1,136,128]{2,1,0:T(8,128)S(1)} %dynamic-slice_add_fusion.2), channel_id=1, source_target_pairs={{0,2},{1,3},{2,0},{3,1},{4,6},{5,7},{6,4},{7,5},{8,10},{9,11},{10,... | collective-permute-start | bytes 208904 | tf_op jit(solution)/shard_map/ppermute | solution.py:18
  11.3 18.7 %collective-permute-start.12 = (bf16[256,1280]{1,0:T(8,128)(2,1)}, bf16[256,1280]{1,0:T(8,128)(2,1)S(1)}, u32[]{:S(2)}, u32[]{:S(2)}) collective-permute-start(bf16[256,1280]{1,0:T(8,128)(2,1)} %pad_maximum_fusion), channel_id=1, source_target_pairs={{4,0},{8,4},{12,8},{16,12},{20,16},{24,20},{28,24},{5,1},{9,5},{13... | collective-permute-start | bytes 1966088 | tf_op jit(solution)/shard_map/ppermute | solution.py:13
  14.6 32.2 %collective-permute-start.5 = (bf16[256,1280]{1,0:T(8,128)(2,1)}, bf16[256,1280]{1,0:T(8,128)(2,1)S(1)}, u32[]{:S(2)}, u32[]{:S(2)}) collective-permute-start(bf16[256,1280]{1,0:T(8,128)(2,1)} %pad_maximum_fusion), channel_id=1, source_target_pairs={{0,16},{4,20},{8,24},{12,28},{1,17},{5,21},{9,25},{13,29},{2,18},{... | collective-permute-start | bytes 1966088 | tf_op jit(solution)/shard_map/ppermute | solution.py:13
  16.6 7.0 %collective-permute-start.3 = (f32[1,272,128]{2,1,0:T(8,128)}, f32[1,272,128]{2,1,0:T(8,128)}, u32[]{:S(2)}, u32[]{:S(2)}) collective-permute-start(f32[1,272,128]{2,1,0:T(8,128)} %pad_maximum_fusion.10), channel_id=1, source_target_pairs={{0,1},{1,0},{2,3},{3,2},{4,5},{5,4},{6,7},{7,6},{8,9},{9,8},{10,11... | collective-permute-start | bytes 417800 | tf_op jit(solution)/shard_map/ppermute | solution.py:18
  16.6 30.6 %collective-permute-start.4 = (bf16[256,1280]{1,0:T(8,128)(2,1)}, bf16[256,1280]{1,0:T(8,128)(2,1)S(1)}, u32[]{:S(2)}, u32[]{:S(2)}) collective-permute-start(bf16[256,1280]{1,0:T(8,128)(2,1)} %pad_maximum_fusion), channel_id=1, source_target_pairs={{12,0},{16,4},{20,8},{24,12},{28,16},{13,1},{17,5},{21,9},{25,13},... | collective-permute-start | bytes 1966088 | tf_op jit(solution)/shard_map/ppermute | solution.py:13
  22.2 32.9 %collective-permute-start.13 = (bf16[256,1280]{1,0:T(8,128)(2,1)}, bf16[256,1280]{1,0:T(8,128)(2,1)S(1)}, u32[]{:S(2)}, u32[]{:S(2)}) collective-permute-start(bf16[256,1280]{1,0:T(8,128)(2,1)} %pad_maximum_fusion), channel_id=1, source_target_pairs={{0,8},{4,12},{8,16},{12,20},{16,24},{20,28},{1,9},{5,13},{9,17},{1... | collective-permute-start | bytes 1966088 | tf_op jit(solution)/shard_map/ppermute | solution.py:13
  57.1 1.6 %collective-permute-start.14 = (f32[2,264,128]{2,1,0:T(8,128)S(1)}, f32[2,264,128]{2,1,0:T(8,128)S(1)}, u32[]{:S(2)}, u32[]{:S(2)}) collective-permute-start(f32[2,264,128]{2,1,0:T(8,128)S(1)} %fusion.3), channel_id=1, source_target_pairs={{0,1},{1,0},{2,3},{3,2},{4,5},{5,4},{6,7},{7,6},{8,9},{9,8},{10,11... | collective-permute-start | bytes 811016 | tf_op jit(solution)/shard_map/ppermute | solution.py:18
  57.4 1.9 %collective-permute-start.6 = (f32[2,264,128]{2,1,0:T(8,128)S(1)}, f32[2,264,128]{2,1,0:T(8,128)S(1)}, u32[]{:S(2)}, u32[]{:S(2)}) collective-permute-start(f32[2,264,128]{2,1,0:T(8,128)S(1)} %fusion.6), channel_id=1, source_target_pairs={{0,1},{1,0},{2,3},{3,2},{4,5},{5,4},{6,7},{7,6},{8,9},{9,8},{10,11... | collective-permute-start | bytes 811016 | tf_op jit(solution)/shard_map/ppermute | solution.py:18
  58.8 6.6 %collective-permute-start.15 = (f32[2,132,128]{2,1,0:T(8,128)S(1)}, f32[2,132,128]{2,1,0:T(8,128)S(1)}, u32[]{:S(2)}, u32[]{:S(2)}) collective-permute-start(f32[2,132,128]{2,1,0:T(8,128)S(1)} %constant_dynamic-slice_fusion), channel_id=1, source_target_pairs={{0,2},{1,3},{2,0},{3,1},{4,6},{5,7},{6,4},{7,5},{8,10},{9,11},{10,... | collective-permute-start | bytes 405512 | tf_op jit(solution)/shard_map/ppermute | solution.py:18
  59.5 8.9 %collective-permute-start.7 = (f32[2,132,128]{2,1,0:T(8,128)S(1)}, f32[2,132,128]{2,1,0:T(8,128)S(1)}, u32[]{:S(2)}, u32[]{:S(2)}) collective-permute-start(f32[2,132,128]{2,1,0:T(8,128)S(1)} %constant_dynamic-slice_fusion.1), channel_id=1, source_target_pairs={{0,2},{1,3},{2,0},{3,1},{4,6},{5,7},{6,4},{7,5},{8,10},{9,11},{10,... | collective-permute-start | bytes 405512 | tf_op jit(solution)/shard_map/ppermute | solution.py:18
  65.4 6.2 %collective-permute-start.16 = (f32[2,132,128]{2,1,0:T(8,128)S(1)}, f32[2,132,128]{2,1,0:T(8,128)S(1)}, u32[]{:S(2)}, u32[]{:S(2)}) collective-permute-start(f32[2,132,128]{2,1,0:T(8,128)S(1)} %dynamic-slice_add_fusion), channel_id=1, source_target_pairs={{0,2},{1,3},{2,0},{3,1},{4,6},{5,7},{6,4},{7,5},{8,10},{9,11},{10,... | collective-permute-start | bytes 405512 | tf_op jit(solution)/shard_map/ppermute | solution.py:18
  68.4 5.1 %collective-permute-start.8 = (f32[2,132,128]{2,1,0:T(8,128)S(1)}, f32[2,132,128]{2,1,0:T(8,128)S(1)}, u32[]{:S(2)}, u32[]{:S(2)}) collective-permute-start(f32[2,132,128]{2,1,0:T(8,128)S(1)} %dynamic-slice_add_fusion.1), channel_id=1, source_target_pairs={{0,2},{1,3},{2,0},{3,1},{4,6},{5,7},{6,4},{7,5},{8,10},{9,11},{10,... | collective-permute-start | bytes 405512 | tf_op jit(solution)/shard_map/ppermute | solution.py:18
  71.6 2.0 %collective-permute-start.17 = (f32[2,264,128]{2,1,0:T(8,128)S(1)}, f32[2,264,128]{2,1,0:T(8,128)S(1)}, u32[]{:S(2)}, u32[]{:S(2)}) collective-permute-start(f32[2,264,128]{2,1,0:T(8,128)S(1)} %pad_maximum_fusion.4), channel_id=1, source_target_pairs={{0,1},{1,0},{2,3},{3,2},{4,5},{5,4},{6,7},{7,6},{8,9},{9,8},{10,11... | collective-permute-start | bytes 811016 | tf_op jit(solution)/shard_map/ppermute | solution.py:18
  73.6 11.6 %collective-permute-start.9 = (f32[2,264,128]{2,1,0:T(8,128)S(1)}, f32[2,264,128]{2,1,0:T(8,128)S(1)}, u32[]{:S(2)}, u32[]{:S(2)}) collective-permute-start(f32[2,264,128]{2,1,0:T(8,128)S(1)} %pad_maximum_fusion.1), channel_id=1, source_target_pairs={{0,1},{1,0},{2,3},{3,2},{4,5},{5,4},{6,7},{7,6},{8,9},{9,8},{10,11... | collective-permute-start | bytes 811016 | tf_op jit(solution)/shard_map/ppermute | solution.py:18
  74.3 15.0 %collective-permute-start.19 = (f32[257,256]{1,0:T(8,128)S(1)}, f32[257,256]{1,0:T(8,128)S(1)}, u32[]{:S(2)}, u32[]{:S(2)}) collective-permute-start(f32[257,256]{1,0:T(8,128)S(1)} %pad_maximum_fusion.6), channel_id=1, source_target_pairs={{8,0},{12,4},{16,8},{20,12},{24,16},{28,20},{9,1},{13,5},{17,9},{2... | collective-permute-start | bytes 789512 | tf_op jit(solution)/shard_map/ppermute | solution.py:13
  82.6 11.4 %collective-permute-start.18 = (f32[257,256]{1,0:T(8,128)S(1)}, f32[257,256]{1,0:T(8,128)S(1)}, u32[]{:S(2)}, u32[]{:S(2)}) collective-permute-start(f32[257,256]{1,0:T(8,128)S(1)} %pad_maximum_fusion.5), channel_id=1, source_target_pairs={{0,4},{4,8},{8,12},{12,16},{16,20},{20,24},{24,28},{1,5},{5,9},{9,... | collective-permute-start | bytes 789512 | tf_op jit(solution)/shard_map/ppermute | solution.py:13
  86.0 8.6 %collective-permute-start.11 = (f32[257,256]{1,0:T(8,128)S(1)}, f32[257,256]{1,0:T(8,128)S(1)}, u32[]{:S(2)}, u32[]{:S(2)}) collective-permute-start(f32[257,256]{1,0:T(8,128)S(1)} %pad_maximum_fusion.3), channel_id=1, source_target_pairs={{16,0},{20,4},{24,8},{28,12},{17,1},{21,5},{25,9},{29,13},{18,2},{... | collective-permute-start | bytes 789512 | tf_op jit(solution)/shard_map/ppermute | solution.py:13
  87.4 17.9 %collective-permute-start.10 = (f32[257,256]{1,0:T(8,128)S(1)}, f32[257,256]{1,0:T(8,128)S(1)}, u32[]{:S(2)}, u32[]{:S(2)}) collective-permute-start(f32[257,256]{1,0:T(8,128)S(1)} %pad_maximum_fusion.2), channel_id=1, source_target_pairs={{0,12},{4,16},{8,20},{12,24},{16,28},{1,13},{5,17},{9,21},{13,25},... | collective-permute-start | bytes 789512 | tf_op jit(solution)/shard_map/ppermute | solution.py:13
